TPU v7x, 256 devices: a whole 4x4x8 slice. The times are simulated.
256 devices in a mesh: rows: 64 (over y, z, core), freq: 4 (over x).
Axes of the slice: x: 4, y: 4, z: 8, core: 2. Of those that a mesh axis runs over, the one named last changes fastest.
Arguments:
- snapshots: bfloat16 [1048576, 512], P('rows', 'freq'), may hold values from -60 to 60
- block_cols: int32 [8192, 3], P('rows'), may hold values from 0 to 8191, as said below
- mass_blocks: bfloat16 [8192, 3, 128, 128], P('rows'), may hold values from -2 to 2
- start_group: float32 [512, 32], P('freq'), may hold values from -6 to 6
- start_merge: float32 [64, 32], replicated, may hold values from -6 to 6
Outputs:
- modes: float32 [32, 1048576], P(None, ('rows', 'freq'))
Inputs may be any that keep to these rules, and one draw needn't show every extreme that they name: block_cols[b, 0] is b; the other entries lie within 2 of b, differ from b, and may repeat near the ends.
All inputs are finite; a program needn't handle non-finite values.
Results may differ from a plain program's by a relative error of at most 0.0003.
Values may be sent and summed in bfloat16 or wider, within the bound.
No kernel may reach another device: no remote copies, remote signals or barrier semaphores. Data moves between devices by JAX's collectives and lax.ppermute only.
A program may use at most 128 MiB of HBM per device.

v0:
```python
import jax
import jax.numpy as jnp
from jax import lax
from jax.sharding import PartitionSpec as P

HB = 2
POWER = 2
HIGHEST = lax.Precision.HIGHEST


def extended_2(block, sides, width):
    for axis, dim in sides:
        count = lax.axis_size(axis)
        forward = [(i, i + 1) for i in range(count - 1)]
        backward = [(target, source) for source, target in forward]
        low = lax.ppermute(
            lax.slice_in_dim(block, block.shape[dim] - width, None, axis=dim), axis, forward
        )
        high = lax.ppermute(lax.slice_in_dim(block, 0, width, axis=dim), axis, backward)
        block = jnp.concatenate([low, block, high], axis=dim)
    return block


def orthonormal(columns_block):
    inner_gram = jnp.dot(columns_block.T, columns_block, precision=HIGHEST)
    lower_factor = jnp.linalg.cholesky(inner_gram)
    return lax.linalg.triangular_solve(
        lower_factor, columns_block, left_side=False, lower=True, transpose_a=True
    )


def subspace(gram_matrix, start_block):
    current = start_block
    for repeat in range(POWER):
        current = orthonormal(jnp.dot(gram_matrix, current, precision=HIGHEST))
    return current


def coefficient_tree(full_gram, start_merge, rank_size, freq_count):
    pairs = freq_count // 2
    width = 2 * rank_size
    blocks = jnp.stack(
        [full_gram[p * width : (p + 1) * width, p * width : (p + 1) * width] for p in range(pairs)]
    )
    pair_weights = jax.vmap(subspace, in_axes=(0, None))(blocks, start_merge)
    zero = jnp.zeros((width, rank_size), jnp.float32)
    coefficients = []
    for p in range(pairs):
        parts = [zero] * pairs
        parts[p] = pair_weights[p]
        coefficients.append(jnp.concatenate(parts, axis=0))
    while len(coefficients) > 1:
        merged = []
        for position in range(0, len(coefficients), 2):
            joined = jnp.concatenate([coefficients[position], coefficients[position + 1]], axis=1)
            pair_gram = jnp.dot(
                joined.T, jnp.dot(full_gram, joined, precision=HIGHEST), precision=HIGHEST
            )
            merged.append(jnp.dot(joined, subspace(pair_gram, start_merge), precision=HIGHEST))
        coefficients = merged
    return coefficients[0]


def shards(snapshots, block_cols, mass_blocks, start_group, start_merge):
    block_size = mass_blocks.shape[2]
    local_blocks = block_cols.shape[0]
    local_cols = snapshots.shape[1]
    total_rows = lax.axis_size("rows") * snapshots.shape[0]
    extended = extended_2(snapshots, (("rows", 0),), HB * block_size)
    tile_stack = extended.reshape(local_blocks + 2 * HB, block_size, local_cols)
    local_index = block_cols - lax.axis_index("rows") * local_blocks + HB
    picked = tile_stack[local_index]
    weighted = jnp.einsum("bkij,bkjc->bic", mass_blocks, picked, preferred_element_type=jnp.float32)
    weighted = weighted.reshape(local_blocks * block_size, local_cols)
    local_gram = jnp.dot(weighted.T, weighted, precision=HIGHEST)
    group_gram = lax.psum(local_gram, "rows") / total_rows
    weights = subspace(group_gram, start_group)
    modes = lax.dot_general(weights, weighted, (((0,), (1,)), ((), ())), precision=HIGHEST)
    rank_size = modes.shape[0]
    freq_count = lax.axis_size("freq")
    quarter = lax.all_to_all(modes, "freq", 1, 0, tiled=True)
    full_gram = (
        lax.psum(jnp.dot(quarter, quarter.T, precision=HIGHEST), ("rows", "freq")) / total_rows
    )
    combined = coefficient_tree(full_gram, start_merge, rank_size, freq_count)
    result = jnp.dot(combined.T, quarter, precision=HIGHEST)
    return result


def solution(mesh):
    in_specs = (
        P("rows", "freq"),
        P("rows", None),
        P("rows", None, None, None),
        P("freq", None),
        P(),
    )
    out_specs = P(None, ("rows", "freq"))
    return jax.shard_map(shards, mesh=mesh, in_specs=in_specs, out_specs=out_specs, check_vma=False)
```

profile of v0, /device:TPU:1, one launch (start us, length us, event | category | flops | bytes accessed | tf_op | source)
XLA Modules:
  0.0 596.8 jit_solution(17205891390755514347)
XLA Ops:
  6.5 0.9 fusion.50
  7.4 4.9 collective-permute-start
  12.4 1.9 collective-permute-start.1
  14.3 0.7 compare_select_fusion
  15.3 2.6 collective-permute-done.1
  18.0 10.8 %pad_maximum_fusion = bf16[16896,128]{1,0:T(8,128)(2,1)} fusion(bf16[256,128]{1,0:T(8,128)(2,1)S(1)} %collective-permute-done.1, bf16[16384,128]{1,0:T(8,128)(2,1)} %param.13, bf16[256,128]{1,0:T(8,128)(2,1)S(1)} %collective-permute-done), kind=kLoop, calls=%fused_computation.3 | loop fusion | flops 12976128 | bytes 8650752 | tf_op jit(solution)/shard_map/concatenate | solution.py:20
  28.7 13.6 %gather_fusion = bf16[384,128,128]{2,1,0:T(8,128)(2,1)} fusion(bf16[132,128,128]{2,1,0:T(8,128)(2,1)} %bitcast.133, s32[1024]{0:T(1024)S(1)} %pad_clamp_fusion), kind=kCustom, calls=%fused_computation | custom fusion | bytes 25167360 | tf_op jit(solution)/shard_map/gather | solution.py:72
  42.3 14.8 %fusion.62 = f32[128,128,128,1]{1,2,3,0:T(8,128)} fusion(bf16[128,3,128,128]{3,2,1,0:T(8,128)(2,1)} %param.15, bf16[128,3,128,128]{3,2,1,0:T(8,128)(2,1)} %bitcast.132), kind=kOutput, calls=%fused_computation.103 | convolution fusion | flops 1610612736 | bytes 33554432 | tf_op jit(solution)/shard_map/bkij,bkjc->bic/dot_general | solution.py:73
  57.1 17.6 %fusion.2 = f32[128,128]{1,0:T(8,128)} fusion(f32[128,128,128,1]{1,2,3,0:T(8,128)} %fusion.62), kind=kOutput, calls=%fused_computation.4 | convolution fusion | flops 3221225472 | bytes 8454144 | tf_op jit(solution)/shard_map/dot_general | solution.py:75
  74.7 173.3 %all-reduce.5.cloned.1.call-done = f32[128,128]{1,0:T(8,128)} async-done(((f32[128,128]{1,0:T(8,128)}), f32[128,128]{1,0:T(8,128)}) %all-reduce.5.cloned.1.call-update) | async-done | bytes 65552 | tf_op jit(solution)/shard_map/psum | solution.py:76
  248.0 1.0 fusion.7
  249.3 2.9 cholesky.117
  252.3 0.6 compare_reduce_fusion.5
  252.9 0.7 fusion.17
  253.6 2.4 custom-call.18
  256.0 0.2 convolution_bitcast_fusion.5
  256.3 1.0 fusion.5
  257.6 2.9 cholesky.128
  260.5 0.6 compare_reduce_fusion.4
  261.2 0.7 fusion.18
  261.8 2.4 custom-call.19
  264.3 0.2 convolution_bitcast_fusion.4
  264.5 13.0 %fusion.53 = f32[32,4,4096]{2,0,1:T(8,128)} fusion(f32[128,32,1]{0,1,2:T(8,128)S(1)} %convolution_bitcast_fusion.4, f32[4,4096,128]{2,1,0:T(8,128)} %bitcast.131), kind=kOutput, calls=%fused_computation.94 | convolution fusion | flops 805306368 | bytes 10502144 | tf_op jit(solution)/shard_map/dot_general | solution.py:78
  277.5 4.0 all-to-all-start
  281.5 25.8 %all-to-all-done = f32[32,4,4096]{2,0,1:T(8,128)S(1)} async-done(((f32[32,4,4096]{2,0,1:T(8,128)}), f32[32,4,4096]{2,0,1:T(8,128)S(1)}, u32[]{:S(2)}, u32[]{:S(2)}) %all-to-all-start) | async-done | bytes 2097184 | tf_op jit(solution)/shard_map/all_to_all | solution.py:81
  307.2 2.4 fusion.54
  309.7 237.2 %all-reduce.7.cloned.1.call-done = f32[128,128]{1,0:T(8,128)} async-done(((f32[128,128]{1,0:T(8,128)}), f32[128,128]{1,0:T(8,128)}) %all-reduce.7.cloned.1.call-update) | async-done | bytes 65552 | tf_op jit(solution)/shard_map/psum | solution.py:83
  546.9 0.8 broadcast_multiply_fusion
  547.8 0.3 fusion.10
  548.4 6.1 %custom-call.20 = f32[2,32,32]{2,1,0:T(8,128)S(1)} custom-call(f32[2,32,32]{2,1,0:T(8,128)S(1)} %fusion.14), custom_call_target="Cholesky" | custom-call | tf_op jit(solution)/shard_map/vmap(jit(cholesky))/cholesky | solution.py:26
  554.8 4.9 custom-call.21
  559.7 0.3 convolution_bitcast_fusion.1
  560.5 5.9 custom-call.22
  566.6 4.9 custom-call.23
  571.5 0.3 convolution_bitcast_fusion
  571.8 1.1 fusion.36
  572.8 0.2 fusion.35
  573.5 2.9 cholesky.161
  576.5 0.6 compare_reduce_fusion.1
  577.1 0.7 fusion.19
  577.8 2.4 custom-call.24
  580.2 0.2 convolution_bitcast_fusion.3
  580.9 2.9 cholesky.172
  583.8 0.6 compare_reduce_fusion
  584.5 0.7 fusion.20
  585.1 2.4 custom-call.25
  587.6 0.2 convolution_bitcast_fusion.2
  588.0 2.0 fusion.61
  (48 shorter events, 3.3 us)
Async XLA Ops:
  6.5 541.3 %copy-start = (f32[64,32]{0,1:T(8,128)S(1)}, f32[64,32]{0,1:T(8,128)}, u32[]{:S(2)}) copy-start(f32[64,32]{0,1:T(8,128)} %param.17) | copy-start | bytes 24580
  6.5 241.5 %all-reduce.5.cloned.1.call-start = ((), (), s32[]{:S(2)}) async-start(), calls=%async_computation.1 | async-start | bytes 131072 | tf_op jit(solution)/shard_map/psum | solution.py:76
  7.4 7.9 %collective-permute-start = (bf16[256,128]{1,0:T(8,128)(2,1)S(1)}, bf16[256,128]{1,0:T(8,128)(2,1)S(1)}, u32[]{:S(2)}, u32[]{:S(2)}) collective-permute-start(bf16[256,128]{1,0:T(8,128)(2,1)S(1)} %get-tuple-element.6), channel_id=1, source_target_pairs={{0,4},{4,8},{8,12},{12,16},{16,20},{20,24},{24,28},{28,32},{32,36}... | collective-permute-start | bytes 196616 | tf_op jit(solution)/shard_map/ppermute | solution.py:16
  12.4 5.6 collective-permute-start.1
  57.1 191.0 %copy-start.1 = (f32[128,32]{0,1:T(8,128)S(1)}, f32[128,32]{0,1:T(8,128)}, u32[]{:S(2)}) copy-start(f32[128,32]{0,1:T(8,128)} %param.16) | copy-start | bytes 49156
  277.5 29.7 %all-to-all-start = ((f32[32,4,4096]{2,0,1:T(8,128)}), f32[32,4,4096]{2,0,1:T(8,128)S(1)}, u32[]{:S(2)}, u32[]{:S(2)}) async-start(f32[32,4,4096]{2,0,1:T(8,128)} %fusion.53), calls=%async_computation | async-start | bytes 4194304 | tf_op jit(solution)/shard_map/all_to_all | solution.py:81
  281.5 265.5 %all-reduce.7.cloned.1.call-start = ((), (), s32[]{:S(2)}) async-start(), calls=%async_computation.2 | async-start | bytes 131072 | tf_op jit(solution)/shard_map/psum | solution.py:83
Sparse Core Ops, SparseCore 0:
  74.8 173.1 all-reduce.4
  309.8 237.0 all-reduce.6
where the time goes:
time: 597 us
  waiting for transfers between devices  439 us (74%)
  other arithmetic  61.4 us (10%)
  matrix products  56.6 us (9%)
  local copies, waits for them, and re-layouts  15.3 us (3%)
  between operations  13.7 us (2%)
  starting transfers between devices  10.8 us (2%)
    psum x1, waiting for transfers between devices, shards(): lax.psum(jnp.dot(quarter, quarter.T, precision=HIGHEST), ('rows', 'freq'))  237 us
    psum x1, waiting for transfers between devices, shards(): group_gram = lax.psum(local_gram, 'rows') / total_rows  173 us
    another operation x19, other arithmetic, orthonormal(): lower_factor = jnp.linalg.cholesky(inner_gram)  26.7 us
    all_to_all x1, waiting for transfers between devices, shards(): quarter = lax.all_to_all(modes, 'freq', 1, 0, tiled=True)  25.8 us
    another operation x13, other arithmetic, orthonormal(): lax.linalg.triangular_solve(lower_factor, columns_block, left_side=False,...  22.3 us
    dot_general x1, matrix products, shards(): local_gram = jnp.dot(weighted.T, weighted, precision=HIGHEST)  17.6 us
    dot_general x1, matrix products, shards(): jnp.einsum('bkij,bkjc->bic', mass_blocks, picked, preferred_element_type=...  14.8 us
    gather x1, local copies, waits for them, and re-layouts, shards(): picked = tile_stack[local_index]  13.6 us
  transfers between devices with their start and end apart: 5, of which 4 were waited for; matrix products, arithmetic and copies ran while one was open for 0% of the time, Pallas kernels for 0%

commit v1 on v0

--- a/solution.py
+++ b/solution.py
@@ -78,7 +78,10 @@
     modes = lax.dot_general(weights, weighted, (((0,), (1,)), ((), ())), precision=HIGHEST)
     rank_size = modes.shape[0]
     freq_count = lax.axis_size("freq")
-    quarter = lax.all_to_all(modes, "freq", 1, 0, tiled=True)
+    quarter = jnp.concatenate(
+        lax.all_to_all(jnp.stack(jnp.split(modes, lax.axis_size("freq"), axis=1)), "freq", 0, 0),
+        axis=0,
+    )
     full_gram = (
         lax.psum(jnp.dot(quarter, quarter.T, precision=HIGHEST), ("rows", "freq")) / total_rows
     )

time: 597 us -> 597 us (level)
  no operation moved by 1% of the time
where the time goes in v1:
time: 597 us; the launch traced here: 596 us
  waiting for transfers between devices  439 us (74%)
  other arithmetic  62.7 us (11%)
  matrix products  54.6 us (9%)
  local copies, waits for them, and re-layouts  15.5 us (3%)
  between operations  13.7 us (2%)
  starting transfers between devices  10.8 us (2%)
    psum x1, waiting for transfers between devices, shards(): lax.psum(jnp.dot(quarter, quarter.T, precision=HIGHEST), ('rows', 'freq'))  237 us
    psum x1, waiting for transfers between devices, shards(): group_gram = lax.psum(local_gram, 'rows') / total_rows  173 us
    another operation x19, other arithmetic, orthonormal(): lower_factor = jnp.linalg.cholesky(inner_gram)  26.4 us
    all_to_all x1, waiting for transfers between devices, shards(): lax.all_to_all(jnp.stack(jnp.split(modes, lax.axis_size('freq'), axis=1))...  25.8 us
    another operation x13, other arithmetic, orthonormal(): lax.linalg.triangular_solve(lower_factor, columns_block, left_side=False,...  22.3 us
    dot_general x1, matrix products, shards(): local_gram = jnp.dot(weighted.T, weighted, precision=HIGHEST)  17.6 us
    dot_general x1, matrix products, shards(): jnp.einsum('bkij,bkjc->bic', mass_blocks, picked, preferred_element_type=...  14.8 us
    gather x1, local copies, waits for them, and re-layouts, shards(): picked = tile_stack[local_index]  13.6 us
  transfers between devices with their start and end apart: 5, of which 4 were waited for; matrix products, arithmetic and copies ran while one was open for 0% of the time, Pallas kernels for 0%

profile of v1, /device:TPU:1, one launch (start us, length us, event | category | flops | bytes accessed | tf_op | source)
XLA Modules:
  0.0 596.1 jit_solution(16974677134353535647)
XLA Ops:
  6.5 0.9 fusion.50
  7.4 4.9 collective-permute-start
  12.4 1.9 collective-permute-start.1
  14.3 0.7 compare_select_fusion
  15.3 2.6 collective-permute-done.1
  18.0 10.8 %pad_maximum_fusion = bf16[16896,128]{1,0:T(8,128)(2,1)} fusion(bf16[256,128]{1,0:T(8,128)(2,1)S(1)} %collective-permute-done.1, bf16[16384,128]{1,0:T(8,128)(2,1)} %param.13, bf16[256,128]{1,0:T(8,128)(2,1)S(1)} %collective-permute-done), kind=kLoop, calls=%fused_computation.3 | loop fusion | flops 12976128 | bytes 8650752 | tf_op jit(solution)/shard_map/concatenate | solution.py:20
  28.7 13.6 %gather_fusion = bf16[384,128,128]{2,1,0:T(8,128)(2,1)} fusion(bf16[132,128,128]{2,1,0:T(8,128)(2,1)} %bitcast.137, s32[1024]{0:T(1024)S(1)} %pad_clamp_fusion), kind=kCustom, calls=%fused_computation | custom fusion | bytes 25167360 | tf_op jit(solution)/shard_map/gather | solution.py:72
  42.3 14.8 %fusion.62 = f32[128,128,128,1]{1,2,3,0:T(8,128)} fusion(bf16[128,3,128,128]{3,2,1,0:T(8,128)(2,1)} %param.15, bf16[128,3,128,128]{3,2,1,0:T(8,128)(2,1)} %bitcast.136), kind=kOutput, calls=%fused_computation.108 | convolution fusion | flops 1610612736 | bytes 33554432 | tf_op jit(solution)/shard_map/bkij,bkjc->bic/dot_general | solution.py:73
  57.1 17.6 %fusion.2 = f32[128,128]{1,0:T(8,128)} fusion(f32[128,128,128,1]{1,2,3,0:T(8,128)} %fusion.62), kind=kOutput, calls=%fused_computation.5 | convolution fusion | flops 3221225472 | bytes 8454144 | tf_op jit(solution)/shard_map/dot_general | solution.py:75
  74.7 173.3 %all-reduce.5.cloned.1.call-done = f32[128,128]{1,0:T(8,128)} async-done(((f32[128,128]{1,0:T(8,128)}), f32[128,128]{1,0:T(8,128)}) %all-reduce.5.cloned.1.call-update) | async-done | bytes 65552 | tf_op jit(solution)/shard_map/psum | solution.py:76
  248.0 1.0 fusion.7
  249.3 2.9 cholesky.117
  252.3 0.6 compare_reduce_fusion.5
  252.9 0.7 fusion.17
  253.6 2.4 custom-call.18
  256.0 0.2 convolution_bitcast_fusion.5
  256.3 1.0 fusion.5
  257.6 2.9 cholesky.128
  260.5 0.6 compare_reduce_fusion.4
  261.2 0.7 fusion.18
  261.8 2.4 custom-call.19
  264.3 0.2 convolution_bitcast_fusion.4
  264.5 10.9 %fusion.53 = f32[32,16384]{1,0:T(8,128)S(1)} fusion(f32[128,32]{0,1:T(8,128)S(1)} %convolution_bitcast_fusion.4, f32[16384,128]{1,0:T(8,128)} %bitcast.135), kind=kOutput, calls=%fused_computation.99 | convolution fusion | flops 805306368 | bytes 10502144 | tf_op jit(solution)/shard_map/dot_general | solution.py:78
  275.6 1.5 pad_maximum_fusion.1
  277.1 4.0 all-to-all-start
  281.1 25.8 %all-to-all-done = f32[4,32,4096]{2,1,0:T(8,128)S(1)} async-done(((f32[4,32,4096]{2,1,0:T(8,128)}), f32[4,32,4096]{2,1,0:T(8,128)S(1)}, u32[]{:S(2)}, u32[]{:S(2)}) %all-to-all-start) | async-done | bytes 2097184 | tf_op jit(solution)/shard_map/all_to_all | solution.py:82
  306.8 2.4 fusion.54
  309.3 237.2 %all-reduce.7.cloned.1.call-done = f32[128,128]{1,0:T(8,128)} async-done(((f32[128,128]{1,0:T(8,128)}), f32[128,128]{1,0:T(8,128)}) %all-reduce.7.cloned.1.call-update) | async-done | bytes 65552 | tf_op jit(solution)/shard_map/psum | solution.py:86
  546.5 0.8 broadcast_multiply_fusion
  547.4 0.3 fusion.10
  548.0 5.9 custom-call.20
  554.1 4.9 custom-call.21
  559.0 0.3 convolution_bitcast_fusion.1
  559.8 5.9 custom-call.22
  565.9 4.9 custom-call.23
  570.8 0.3 convolution_bitcast_fusion
  571.1 1.1 fusion.36
  572.8 2.9 cholesky.161
  575.8 0.6 compare_reduce_fusion.1
  576.4 0.7 fusion.19
  577.1 2.4 custom-call.24
  579.5 0.2 convolution_bitcast_fusion.3
  580.2 2.9 cholesky.172
  583.1 0.6 compare_reduce_fusion
  583.8 0.7 fusion.20
  584.4 2.4 custom-call.25
  586.9 0.2 convolution_bitcast_fusion.2
  587.3 2.0 fusion.61
  (50 shorter events, 3.7 us)
Async XLA Ops:
  6.5 540.9 %copy-start = (f32[64,32]{0,1:T(8,128)S(1)}, f32[64,32]{0,1:T(8,128)}, u32[]{:S(2)}) copy-start(f32[64,32]{0,1:T(8,128)} %param.17) | copy-start | bytes 24580
  6.5 241.5 %all-reduce.5.cloned.1.call-start = ((), (), s32[]{:S(2)}) async-start(), calls=%async_computation.1 | async-start | bytes 131072 | tf_op jit(solution)/shard_map/psum | solution.py:76
  7.4 7.9 %collective-permute-start = (bf16[256,128]{1,0:T(8,128)(2,1)S(1)}, bf16[256,128]{1,0:T(8,128)(2,1)S(1)}, u32[]{:S(2)}, u32[]{:S(2)}) collective-permute-start(bf16[256,128]{1,0:T(8,128)(2,1)S(1)} %get-tuple-element.6), channel_id=1, source_target_pairs={{0,4},{4,8},{8,12},{12,16},{16,20},{20,24},{24,28},{28,32},{32,36}... | collective-permute-start | bytes 196616 | tf_op jit(solution)/shard_map/ppermute | solution.py:16
  12.4 5.6 collective-permute-start.1
  57.1 191.0 %copy-start.1 = (f32[128,32]{0,1:T(8,128)S(1)}, f32[128,32]{0,1:T(8,128)}, u32[]{:S(2)}) copy-start(f32[128,32]{0,1:T(8,128)} %param.16) | copy-start | bytes 49156
  277.1 29.7 %all-to-all-start = ((f32[4,32,4096]{2,1,0:T(8,128)}), f32[4,32,4096]{2,1,0:T(8,128)S(1)}, u32[]{:S(2)}, u32[]{:S(2)}) async-start(f32[4,32,4096]{2,1,0:T(8,128)} %pad_maximum_fusion.1), calls=%async_computation | async-start | bytes 4194304 | tf_op jit(solution)/shard_map/all_to_all | solution.py:82
  281.0 265.4 %all-reduce.7.cloned.1.call-start = ((), (), s32[]{:S(2)}) async-start(), calls=%async_computation.2 | async-start | bytes 131072 | tf_op jit(solution)/shard_map/psum | solution.py:86
Sparse Core Ops, SparseCore 0:
  74.8 173.1 all-reduce.4
  309.4 237.0 all-reduce.6
